TPU v7x, 128 devices: a whole 4x4x4 slice. The times are simulated.
128 devices in a mesh: sec: 2 (over y_hi), seq: 8 (over x, core), trk: 8 (over y_lo, z).
Axes of the slice: x: 4, y: 4 (y_hi: 2, y_lo: 2; y = y_hi * 2 + y_lo), z: 4, core: 2. Of those that a mesh axis runs over, the one named last changes fastest.
Arguments:
- tokens: bfloat16 [8, 512, 1536], P('sec', 'seq'), may hold values from -6 to 6
- norm_gain: bfloat16 [1536], replicated, may hold values from 0.25 to 1.75
- dilated_conv_weight: bfloat16 [1536, 3, 1536], P(None, None, 'trk'), may hold values from -0.09375 to 0.09375
- head_weight: bfloat16 [1536, 8, 20, 128], P(None, 'trk'), may hold values from -0.15625 to 0.15625
- targets: bfloat16 [8, 512, 8, 20, 128], P('sec', 'seq', 'trk'), may hold values from 0 to 2
- owner_tiles: int32 [8, 20], P('trk'), may hold values from -1 to 80, as said below
- species: int32 [8], P('sec'), may hold values from 0 to 1, as said below
Outputs:
- conv_grad: float32 [1536, 3, 1536], P(('sec', 'seq'), None, 'trk')
- head_grad: float32 [1536, 8, 20, 128], P(('sec', 'seq'), 'trk')
Inputs may be any that keep to these rules, and one draw needn't show every extreme that they name: `owner_tiles`: each of the 81 tiles (human tiles 0 to 59, then the mouse tiles) stands in exactly one slot of one owner; -1 marks an empty slot; in every draw one owner has all 20 slots filled. `species`: 0 is human, 1 is mouse; exactly half of the samples are mouse.
All inputs are finite; a program needn't handle non-finite values.
Results may differ from a plain program's by a relative error of at most 0.0023.
Values may be sent and summed in bfloat16 or wider, within the bound.
No kernel may reach another device: no remote copies, remote signals or barrier semaphores. Data moves between devices by JAX's collectives and lax.ppermute only.
A program may use at most 128 MiB of HBM per device.

v0:
```python
import math
import jax
import jax.numpy as jnp
from jax import lax
from jax.sharding import PartitionSpec as P

HTRACKS = 7611
MTRACKS = 2608
DILATION_BINS = 16
HTILES = 60
grad_clip = 0.1


def padded(cells, sides, width):
    for axis, dim in sides:
        count = lax.axis_size(axis)
        ends = count - 1
        head = lax.slice_in_dim(cells, 0, width, axis=dim)
        tail = lax.slice_in_dim(cells, cells.shape[dim] - width, cells.shape[dim], axis=dim)
        cells = jnp.concatenate(
            [
                lax.ppermute(tail, axis, [(i, (i + 1) % count) for i in range(ends)]),
                cells,
                lax.ppermute(head, axis, [((i + 1) % count, i) for i in range(ends)]),
            ],
            axis=dim,
        )
    return cells


def contracted_rows(left, right):
    return lax.dot_general(
        left, right, (((0,), (0,)), ((), ())), preferred_element_type=jnp.float32
    )


def body(tokens, norm_gain, dilated_conv_weight, head_weight, targets, owner_tiles, species):
    sample_count = tokens.shape[0]
    local_rows = tokens.shape[1]
    width_all = tokens.shape[2]
    tap_count = dilated_conv_weight.shape[1]
    out_share = dilated_conv_weight.shape[2]
    slot_count = head_weight.shape[2]
    lane_count = head_weight.shape[3]
    inputs = tokens.astype(jnp.float32)
    mean_sq = jnp.mean(inputs * inputs, axis=-1, keepdims=True)
    normed = inputs * lax.rsqrt(mean_sq + 1e-06) * norm_gain.astype(jnp.float32)
    hidden_state = jax.nn.gelu(normed).astype(jnp.bfloat16)
    padded_input = padded(hidden_state, (("seq", 1),), DILATION_BINS)
    convolution_output = jnp.zeros((sample_count, local_rows, out_share), jnp.float32)
    for kernel_tap_index in range(tap_count):
        convolution_output = convolution_output + jnp.dot(
            padded_input[
                :, kernel_tap_index * DILATION_BINS : kernel_tap_index * DILATION_BINS + local_rows
            ],
            dilated_conv_weight[:, kernel_tap_index, :],
            preferred_element_type=jnp.float32,
        )
    own_cols = lax.dynamic_slice_in_dim(inputs, lax.axis_index("trk") * out_share, out_share, 2)
    mixed_share = (own_cols + convolution_output).astype(jnp.bfloat16)
    mixed_all = lax.all_gather(mixed_share, "trk", axis=2, tiled=True)
    tiles_here = owner_tiles[0]
    is_mouse = tiles_here >= HTILES
    within = jnp.where(is_mouse, tiles_here - HTILES, tiles_here)
    track_limit = jnp.where(is_mouse, MTRACKS, HTRACKS).astype(jnp.int32)
    lane_ids = jnp.arange(lane_count, dtype=jnp.int32)
    lane_mask = (within[:, None] * lane_count + lane_ids[None, :] < track_limit[:, None]).astype(
        jnp.float32
    )
    grad_scale = 1.0 / math.sqrt(
        lax.axis_size("sec") * sample_count * lax.axis_size("seq") * local_rows
    )
    weights_here = head_weight[:, 0].reshape(width_all, slot_count * lane_count)
    flat_mixed = mixed_all.reshape(sample_count * local_rows, width_all)
    logits = jnp.dot(flat_mixed, weights_here, preferred_element_type=jnp.float32)
    target_cols = targets[:, :, 0].reshape(sample_count * local_rows, slot_count * lane_count)
    active = (tiles_here[None, :] >= 0) & (is_mouse[None, :] == (species[:, None] == 1))
    live_mask = active.astype(jnp.float32)[:, :, None] * lane_mask[None, :, :]
    live_rows = jnp.broadcast_to(
        live_mask.reshape(sample_count, 1, slot_count * lane_count),
        (sample_count, local_rows, slot_count * lane_count),
    ).reshape(sample_count * local_rows, slot_count * lane_count)
    delta_f = (
        grad_scale
        * (jax.nn.softplus(logits) - target_cols.astype(jnp.float32))
        * jax.nn.sigmoid(logits)
        * live_rows
    )
    flat_deltas = delta_f.astype(jnp.bfloat16)
    back_sum = lax.dot_general(
        flat_deltas, weights_here, (((1,), (1,)), ((), ())), preferred_element_type=jnp.float32
    ).reshape(sample_count, local_rows, width_all)
    backward_portion = lax.psum_scatter(back_sum, "trk", scatter_dimension=2, tiled=True).astype(
        jnp.bfloat16
    )
    group_count = lax.axis_size("sec") * lax.axis_size("seq")
    share_rows = width_all // group_count
    per_tap = [
        lax.dot_general(
            padded_input[
                :, kernel_tap_index * DILATION_BINS : kernel_tap_index * DILATION_BINS + local_rows
            ],
            backward_portion,
            (((0, 1), (0, 1)), ((), ())),
            preferred_element_type=jnp.float32,
        )
        for kernel_tap_index in range(tap_count)
    ]
    conv_grad = lax.psum_scatter(
        jnp.stack(per_tap, axis=1), ("sec", "seq"), scatter_dimension=0, tiled=True
    )
    grad_share = lax.psum_scatter(
        contracted_rows(flat_mixed, flat_deltas), ("sec", "seq"), scatter_dimension=0, tiled=True
    )
    total_sq = lax.psum(jnp.sum(grad_share * grad_share), ("sec", "seq", "trk"))
    entries = width_all * lax.axis_size("trk") * slot_count * lane_count
    factor = jnp.minimum(1.0, grad_clip * lax.rsqrt(total_sq / entries + 1e-06))
    head_grad = (grad_share * factor).reshape(share_rows, 1, slot_count, lane_count)
    return (conv_grad, head_grad)


def solution(mesh):
    return jax.shard_map(
        body,
        mesh=mesh,
        in_specs=(
            P("sec", "seq", None),
            P(),
            P(None, None, "trk"),
            P(None, "trk", None, None),
            P("sec", "seq", "trk", None, None),
            P("trk", None),
            P("sec"),
        ),
        out_specs=(P(("sec", "seq"), None, "trk"), P(("sec", "seq"), "trk", None, None)),
        check_vma=False,
    )
```

profile of v0, /device:TPU:1, one launch (start us, length us, event | category | flops | bytes accessed | tf_op | source)
XLA Modules:
  0.0 435.4 jit_solution(13732311764783962784)
XLA Ops:
  7.2 1.4 multiply_reduce_fusion
  8.7 0.7 convert_element_type.39
  9.4 1.8 fusion.12
  11.2 0.8 fusion.33
  12.0 4.5 %collective-permute-start = (bf16[4,16,1536]{2,1,0:T(8,128)(2,1)}, bf16[4,16,1536]{2,1,0:T(8,128)(2,1)S(1)}, u32[]{:S(2)}, u32[]{:S(2)}) collective-permute-start(bf16[4,16,1536]{2,1,0:T(8,128)(2,1)} %get-tuple-element.10), channel_id=1, source_target_pairs={{0,8},{8,16},{16,24},{24,32},{32,40},{40,48},{48,56},{1,9},{9,17},... | collective-permute-start | bytes 589832 | tf_op jit(solution)/shard_map/ppermute | solution.py:22
  16.5 1.9 collective-permute-start.1
  18.6 0.7 broadcast_compare_fusion
  19.5 3.8 copy.26
  23.3 10.6 %copy.25 = bf16[1536,1,20,128]{0,3,2,1:T(8,128)(2,1)} copy(bf16[1536,1,20,128]{3,0,2,1:T(8,128)(2,1)} %param.10) | data formatting | bytes 15728640 | tf_op args[3]
  34.1 0.6 bitcast_multiply_fusion
  34.7 1.4 fusion.18
  36.6 0.4 fusion.15
  37.1 29.0 %all_gather.3 = bf16[4,64,1536]{1,0,2:T(4,128)(2,1)S(1)} all-gather(bf16[4,64,192]{1,0,2:T(4,128)(2,1)S(1)} %copy.23), channel_id=1, replica_groups=mesh['sec'=2,'seq'=8,'trk'=8] {'trk'}, dimensions={2}, use_global_device_ids=true | all-gather | bytes 884736 | tf_op jit(solution)/shard_map/all_gather | solution.py:61
  66.1 0.9 copy.24
  67.0 8.5 %fusion.4 = bf16[256,2560]{1,0:T(8,128)(2,1)S(1)} fusion(f32[32,8,20,128]{3,2,1,0:T(8,128)} %bitcast.78, f32[4,2560]{1,0:T(4,128)} %bitcast_multiply_fusion, bf16[256,1536]{1,0:T(8,128)(2,1)S(1)} %bitcast.79, bf16[1536,2560]{0,1:T(8,128)(2,1)} %bitcast.74), kind=kOutput, calls=%fused_computation.6 | convolution fusion | flops 2022440960 | bytes 12623872 | tf_op jit(solution)/shard_map/dot_general | solution.py:75
  75.5 1.2 copy-done.3
  76.7 5.4 %fusion.34 = f32[4,64,1536]{2,1,0:T(8,128)S(1)} fusion(bf16[4,64,2560]{2,1,0:T(8,128)(2,1)S(1)} %bitcast.81, bf16[1536,2560,1]{0,1,2:T(8,128)(2,1)} %bitcast.75), kind=kOutput, calls=%fused_computation.59 | convolution fusion | flops 2013265920 | bytes 10747904 | tf_op jit(solution)/shard_map/dot_general | solution.py:90
  82.1 2.7 copy.32
  84.9 4.2 reshape.148
  89.1 41.3 %reduce-scatter.10.cloned.1.call-done = f32[192,256]{1,0:T(8,128)} async-done(((f32[1536,256]{1,0:T(8,128)}), f32[192,256]{1,0:T(8,128)}) %reduce-scatter.10.cloned.1.call-update) | async-done | bytes 196624
  130.4 1.1 reshape.149
  132.9 3.1 copy.36
  136.3 0.9 copy-done.1
  137.2 0.4 copy-done.4
  137.6 7.7 %fusion.35 = f32[1536,2560]{1,0:T(8,128)} fusion(bf16[256,1536]{1,0:T(8,128)(2,1)S(1)} %bitcast.80, bf16[256,2560]{1,0:T(8,128)(2,1)S(1)} %copy-done.4), kind=kOutput, calls=%fused_computation.60 | convolution fusion | flops 2013265920 | bytes 17825792 | tf_op jit(solution)/shard_map/dot_general | solution.py:32
  145.4 71.8 %reduce-scatter.12.cloned.1.call-done = f32[96,576]{1,0:T(8,128)} async-done(((f32[1536,576]{1,0:T(8,128)}), f32[96,576]{1,0:T(8,128)}) %reduce-scatter.12.cloned.1.call-update) | async-done | bytes 221200
  217.2 1.1 copy.37
  218.3 140.2 %reduce-scatter.8.cloned.1.call-done = f32[96,2560]{1,0:T(8,128)} async-done(((f32[1536,2560]{1,0:T(8,128)}), f32[96,2560]{1,0:T(8,128)}) %reduce-scatter.8.cloned.1.call-update) | async-done | bytes 983056 | tf_op jit(solution)/shard_map/reduce_scatter | solution.py:112
  358.4 2.1 multiply_reduce_fusion.1
  360.6 0.9 copy.28
  361.5 64.5 %psum.7 = f32[]{:T(128)} all-reduce(f32[]{:T(128)} %multiply_reduce_fusion.1), channel_id=1, replica_groups=mesh['sec'=2,'seq'=8,'trk'=8] {'sec','seq','trk'}, use_global_device_ids=true, to_apply=%region_5.6 | all-reduce | flops 1 | bytes 8 | tf_op jit(solution)/shard_map/psum | solution.py:115
  426.8 2.1 reshape.147
  (37 shorter events, 2.9 us)
Async XLA Ops:
  7.2 11.3 %copy-start.2 = (bf16[4,64,1536]{2,1,0:T(8,128)(2,1)S(1)}, bf16[4,64,1536]{2,1,0:T(8,128)(2,1)}, u32[]{:S(2)}) copy-start(bf16[4,64,1536]{2,1,0:T(8,128)(2,1)} %param.7) | copy-start | bytes 2359300
  7.2 11.2 %copy-start.7 = (s32[1,20]{1,0:T(1,128)S(1)}, s32[1,20]{1,0:T(1,128)}, u32[]{:S(2)}) copy-start(s32[1,20]{1,0:T(1,128)} %param.12) | copy-start | bytes 244
  7.2 123.2 %reduce-scatter.10.cloned.1.call-start = ((), (), s32[]{:S(2)}) async-start(), calls=%async_computation.4 | async-start | bytes 1769472
  12.0 24.6 %collective-permute-start = (bf16[4,16,1536]{2,1,0:T(8,128)(2,1)}, bf16[4,16,1536]{2,1,0:T(8,128)(2,1)S(1)}, u32[]{:S(2)}, u32[]{:S(2)}) collective-permute-start(bf16[4,16,1536]{2,1,0:T(8,128)(2,1)} %get-tuple-element.10), channel_id=1, source_target_pairs={{0,8},{8,16},{16,24},{24,32},{32,40},{40,48},{48,56},{1,9},{9,17},... | collective-permute-start | bytes 589832 | tf_op jit(solution)/shard_map/ppermute | solution.py:22
  16.5 19.7 %collective-permute-start.1 = (bf16[4,16,1536]{2,1,0:T(8,128)(2,1)}, bf16[4,16,1536]{2,1,0:T(8,128)(2,1)S(1)}, u32[]{:S(2)}, u32[]{:S(2)}) collective-permute-start(bf16[4,16,1536]{2,1,0:T(8,128)(2,1)} %get-tuple-element.11), channel_id=1, source_target_pairs={{8,0},{16,8},{24,16},{32,24},{40,32},{48,40},{56,48},{9,1},{17,9},... | collective-permute-start | bytes 589832 | tf_op jit(solution)/shard_map/ppermute | solution.py:24
  33.9 2.2 copy-start.6
  67.0 8.5 %copy-start = (bf16[4,64,1536]{2,1,0:T(8,128)(2,1)}, bf16[4,64,1536]{2,1,0:T(8,128)(2,1)S(1)}, u32[]{:S(2)}) copy-start(bf16[4,64,1536]{2,1,0:T(8,128)(2,1)S(1)} %copy.24) | copy-start | bytes 2359300
  75.5 1.2 copy-start.3
  89.1 128.1 %reduce-scatter.12.cloned.1.call-start = ((), (), s32[]{:S(2)}) async-start(), calls=%async_computation.5 | async-start | bytes 4177920
  136.0 1.1 copy-start.1
  136.0 1.6 copy-start.4
  136.1 222.4 %reduce-scatter.8.cloned.1.call-start = ((), (), s32[]{:S(2)}) async-start(), calls=%async_computation.3 | async-start | bytes 16711680 | tf_op jit(solution)/shard_map/reduce_scatter | solution.py:112
  358.4 68.2 %copy-start.5 = (f32[96,2560]{1,0:T(8,128)S(1)}, f32[96,2560]{1,0:T(8,128)}, u32[]{:S(2)}) copy-start(f32[96,2560]{1,0:T(8,128)} %reduce-scatter.8.cloned.1.call-done) | copy-start | bytes 2949124
Sparse Core Ops, SparseCore 0:
  89.2 41.1 reduce-scatter.9
  136.2 80.9 reduce-scatter.11
  221.6 136.7 reduce-scatter.7
where the time goes:
time: 436 us; the launch traced here: 435 us
  waiting for transfers between devices  253 us (58%)
  blocking collectives  93.5 us (21%)
  local copies, waits for them, and re-layouts  34.3 us (8%)
  matrix products  24.9 us (6%)
  between operations  14.7 us (3%)
  other arithmetic  7.97 us (2%)
  starting transfers between devices  6.71 us (2%)
    reduce_scatter x1, waiting for transfers between devices, body(): lax.psum_scatter(contracted_rows(flat_mixed, flat_deltas), ('sec', 'seq')...  140 us
    unnamed x5, waiting for transfers between devices  113 us
    psum x1, blocking collectives, body(): total_sq = lax.psum(jnp.sum(grad_share * grad_share), ('sec', 'seq', 'trk'))  64.5 us
    all_gather x1, blocking collectives, body(): mixed_all = lax.all_gather(mixed_share, 'trk', axis=2, tiled=True)  29 us
    unnamed x25, local copies, waits for them, and re-layouts  26.4 us
  transfers between devices with their start and end apart: 5, of which 3 were waited for; matrix products, arithmetic and copies ran while one was open for 6% of the time, Pallas kernels for 0%

commit v1 on v0

--- a/solution.py
+++ b/solution.py
@@ -58,7 +58,9 @@
         )
     own_cols = lax.dynamic_slice_in_dim(inputs, lax.axis_index("trk") * out_share, out_share, 2)
     mixed_share = (own_cols + convolution_output).astype(jnp.bfloat16)
-    mixed_all = lax.all_gather(mixed_share, "trk", axis=2, tiled=True)
+    mixed_all = jnp.concatenate(
+        lax.all_to_all(jnp.stack([mixed_share] * lax.axis_size("trk")), "trk", 0, 0), axis=2
+    )
     tiles_here = owner_tiles[0]
     is_mouse = tiles_here >= HTILES
     within = jnp.where(is_mouse, tiles_here - HTILES, tiles_here)

time: 436 us -> 415 us (0.952)
  blocking collectives: 93.5 us -> 64.4 us
  starting transfers between devices: 6.71 us -> 12.8 us
    all_gather x1 -> x0, blocking collectives: 29 us -> none  [body(): mixed_all = lax.all_gather(mixed_share, 'trk', axis=2, tiled=True)]
    all_to_all x0 -> x1, starting transfers between devices: none -> 6.05 us  [body(): lax.all_to_all(jnp.stack([mixed_share] * lax.axis_size('trk')), 'trk', 0, 0)]
    unnamed x5, waiting for transfers between devices: 113 us -> 109 us
    unnamed x25 -> x31, local copies, waits for them, and re-layouts: 26.4 us -> 28.2 us
  transfers between devices with their start and end apart: 5 -> 6, of which waited for: 3 -> 4; matrix products, arithmetic and copies ran while one was open for 6% -> 7% of each run, Pallas kernels for 0% -> 0%
where the time goes in v1:
time: 415 us; the launch traced here: 414 us
  waiting for transfers between devices  251 us (60%)
  blocking collectives  64.4 us (16%)
  local copies, waits for them, and re-layouts  37.4 us (9%)
  matrix products  27 us (7%)
  between operations  14.7 us (4%)
  starting transfers between devices  12.8 us (3%)
  other arithmetic  7.45 us (2%)
    reduce_scatter x1, waiting for transfers between devices, body(): lax.psum_scatter(contracted_rows(flat_mixed, flat_deltas), ('sec', 'seq')...  140 us
    unnamed x5, waiting for transfers between devices  109 us
    psum x1, blocking collectives, body(): total_sq = lax.psum(jnp.sum(grad_share * grad_share), ('sec', 'seq', 'trk'))  64.4 us
    unnamed x31, local copies, waits for them, and re-layouts  28.2 us
    dot_general x1, matrix products, body(): jnp.dot(flat_mixed, weights_here, preferred_element_type=jnp.float32)  8.41 us
  transfers between devices with their start and end apart: 6, of which 4 were waited for; matrix products, arithmetic and copies ran while one was open for 7% of the time, Pallas kernels for 0%

profile of v1, /device:TPU:1, one launch (start us, length us, event | category | flops | bytes accessed | tf_op | source)
XLA Modules:
  0.0 414.4 jit_solution(247330332789640449)
XLA Ops:
  7.2 1.4 multiply_reduce_fusion
  9.3 1.8 fusion.12
  11.2 4.5 %collective-permute-start = (bf16[4,16,1536]{2,1,0:T(8,128)(2,1)S(1)}, bf16[4,16,1536]{2,1,0:T(8,128)(2,1)S(1)}, u32[]{:S(2)}, u32[]{:S(2)}) collective-permute-start(bf16[4,16,1536]{2,1,0:T(8,128)(2,1)S(1)} %get-tuple-element.8), channel_id=1, source_target_pairs={{0,8},{8,16},{16,24},{24,32},{32,40},{40,48},{48,56},{1,9},{9,17},... | collective-permute-start | bytes 589832 | tf_op jit(solution)/shard_map/ppermute | solution.py:22
  15.7 1.9 collective-permute-start.1
  17.9 1.4 fusion.18
  20.9 1.8 collective-permute-done.1
  22.7 1.4 fusion.16
  24.2 1.5 fusion.15
  25.7 1.1 stack.10
  26.8 6.0 %all-to-all-start = ((bf16[8,4,64,192]{3,2,1,0:T(8,128)(2,1)}), bf16[8,4,64,192]{3,2,1,0:T(8,128)(2,1)S(1)}, u32[]{:S(2)}, u32[]{:S(2)}) async-start(bf16[8,4,64,192]{3,2,1,0:T(8,128)(2,1)} %stack.10), calls=%async_computation | async-start | bytes 2097152 | tf_op jit(solution)/shard_map/all_to_all | solution.py:62
  33.6 2.5 copy.19
  36.1 10.6 %copy.18 = bf16[1536,1,20,128]{0,3,2,1:T(8,128)(2,1)} copy(bf16[1536,1,20,128]{3,0,2,1:T(8,128)(2,1)} %param.10) | data formatting | bytes 15728640 | tf_op args[3]
  46.8 1.0 copy-done.5
  47.8 1.8 copy.17
  49.6 0.9 reshape_reshape.3
  50.5 8.4 %fusion.4 = bf16[256,2560]{1,0:T(8,128)(2,1)S(1)} fusion(f32[32,8,20,128]{3,2,1,0:T(8,128)} %bitcast.80, f32[4,2560]{1,0:T(4,128)S(1)} %bitcast_multiply_fusion, bf16[256,1536]{1,0:T(8,128)(2,1)S(1)} %reshape_reshape.3, bf16[1536,2560]{0,1:T(8,128)(2,1)} %bitcast.76), kind=kOutput, calls=%fused_computation.6 | convolution fusion | flops 2022440960 | bytes 12623872 | tf_op jit(solution)/shard_map/dot_general | solution.py:77
  59.0 1.2 copy-done.3
  60.1 5.4 %fusion.34 = f32[4,64,1536]{2,1,0:T(8,128)S(1)} fusion(bf16[4,64,2560]{2,1,0:T(8,128)(2,1)S(1)} %bitcast.81, bf16[1536,2560,1]{0,1,2:T(8,128)(2,1)} %bitcast.77), kind=kOutput, calls=%fused_computation.59 | convolution fusion | flops 2013265920 | bytes 10747904 | tf_op jit(solution)/shard_map/dot_general | solution.py:92
  65.6 2.7 copy.25
  68.3 4.2 %reshape.150 = f32[1536,256]{1,0:T(8,128)} reshape(f32[1536,4,64]{2,1,0:T(4,128)} %bitcast.79) | data formatting | bytes 3145728
  72.7 36.6 %reduce-scatter.10.cloned.1.call-done = f32[192,256]{1,0:T(8,128)} async-done(((f32[1536,256]{1,0:T(8,128)}), f32[192,256]{1,0:T(8,128)}) %reduce-scatter.10.cloned.1.call-update) | async-done | bytes 196624
  109.3 1.1 reshape.151
  111.8 3.1 copy.29
  115.0 1.1 copy-done.1
  116.5 7.7 %fusion.35 = f32[1536,2560]{1,0:T(8,128)} fusion(bf16[256,1536]{1,0:T(8,128)(2,1)S(1)} %copy-done.1, bf16[256,2560]{1,0:T(8,128)(2,1)S(1)} %copy-done.4), kind=kOutput, calls=%fused_computation.60 | convolution fusion | flops 2013265920 | bytes 17825792 | tf_op jit(solution)/shard_map/dot_general | solution.py:32
  124.3 72.0 %reduce-scatter.12.cloned.1.call-done = f32[96,576]{1,0:T(8,128)} async-done(((f32[1536,576]{1,0:T(8,128)}), f32[96,576]{1,0:T(8,128)}) %reduce-scatter.12.cloned.1.call-update) | async-done | bytes 221200
  196.3 1.1 copy.30
  197.4 140.1 %reduce-scatter.8.cloned.1.call-done = f32[96,2560]{1,0:T(8,128)} async-done(((f32[1536,2560]{1,0:T(8,128)}), f32[96,2560]{1,0:T(8,128)}) %reduce-scatter.8.cloned.1.call-update) | async-done | bytes 983056 | tf_op jit(solution)/shard_map/reduce_scatter | solution.py:114
  337.5 2.1 multiply_reduce_fusion.1
  339.6 0.9 copy.21
  340.5 64.4 %psum.7 = f32[]{:T(128)} all-reduce(f32[]{:T(128)} %multiply_reduce_fusion.1), channel_id=1, replica_groups=mesh['sec'=2,'seq'=8,'trk'=8] {'sec','seq','trk'}, use_global_device_ids=true, to_apply=%region_5.6 | all-reduce | flops 1 | bytes 8 | tf_op jit(solution)/shard_map/psum | solution.py:117
  405.7 2.1 reshape.149
  (45 shorter events, 5.5 us)
Async XLA Ops:
  7.2 10.5 %copy-start.2 = (bf16[4,64,1536]{2,1,0:T(8,128)(2,1)S(1)}, bf16[4,64,1536]{2,1,0:T(8,128)(2,1)}, u32[]{:S(2)}) copy-start(bf16[4,64,1536]{2,1,0:T(8,128)(2,1)} %param.7) | copy-start | bytes 2359300
  7.2 10.5 %copy-start.9 = (s32[1,20]{1,0:T(1,128)S(1)}, s32[1,20]{1,0:T(1,128)}, u32[]{:S(2)}) copy-start(s32[1,20]{1,0:T(1,128)} %param.12) | copy-start | bytes 244
  11.2 6.7 %copy-start.10 = (s32[4]{0:T(128)S(1)}, s32[4]{0:T(128)}, u32[]{:S(2)}) copy-start(s32[4]{0:T(128)} %param.13) | copy-start | bytes 52
  11.2 12.9 %collective-permute-start = (bf16[4,16,1536]{2,1,0:T(8,128)(2,1)S(1)}, bf16[4,16,1536]{2,1,0:T(8,128)(2,1)S(1)}, u32[]{:S(2)}, u32[]{:S(2)}) collective-permute-start(bf16[4,16,1536]{2,1,0:T(8,128)(2,1)S(1)} %get-tuple-element.8), channel_id=1, source_target_pairs={{0,8},{8,16},{16,24},{24,32},{32,40},{40,48},{48,56},{1,9},{9,17},... | collective-permute-start | bytes 589832 | tf_op jit(solution)/shard_map/ppermute | solution.py:22
  15.7 7.0 %collective-permute-start.1 = (bf16[4,16,1536]{2,1,0:T(8,128)(2,1)S(1)}, bf16[4,16,1536]{2,1,0:T(8,128)(2,1)S(1)}, u32[]{:S(2)}, u32[]{:S(2)}) collective-permute-start(bf16[4,16,1536]{2,1,0:T(8,128)(2,1)S(1)} %get-tuple-element.9), channel_id=1, source_target_pairs={{8,0},{16,8},{24,16},{32,24},{40,32},{48,40},{56,48},{9,1},{17,9},... | collective-permute-start | bytes 589832 | tf_op jit(solution)/shard_map/ppermute | solution.py:24
  25.6 7.9 %copy-start.7 = (bf16[4,64,1,20,128]{4,1,3,2,0:T(8,128)(2,1)S(1)}, bf16[4,64,1,20,128]{4,1,3,2,0:T(8,128)(2,1)}, u32[]{:S(2)}) copy-start(bf16[4,64,1,20,128]{4,1,3,2,0:T(8,128)(2,1)} %param.11) | copy-start | bytes 3932164
  26.8 20.0 %all-to-all-start = ((bf16[8,4,64,192]{3,2,1,0:T(8,128)(2,1)}), bf16[8,4,64,192]{3,2,1,0:T(8,128)(2,1)S(1)}, u32[]{:S(2)}, u32[]{:S(2)}) async-start(bf16[8,4,64,192]{3,2,1,0:T(8,128)(2,1)} %stack.10), calls=%async_computation | async-start | bytes 2097152 | tf_op jit(solution)/shard_map/all_to_all | solution.py:62
  32.8 76.5 %reduce-scatter.10.cloned.1.call-start = ((), (), s32[]{:S(2)}) async-start(), calls=%async_computation.5 | async-start | bytes 1769472
  36.1 10.6 %copy-start.8 = (f32[1,4,20,128]{3,2,1,0:T(8,128)S(1)}, f32[1,4,20,128]{3,2,1,0:T(8,128)}, u32[]{:S(2)}) copy-start(f32[1,4,20,128]{3,2,1,0:T(8,128)} %broadcast_bitcast_fusion) | copy-start | bytes 122884
  46.8 1.0 copy-start.5
  50.5 8.4 %copy-start = (bf16[256,1536]{1,0:T(8,128)(2,1)}, bf16[256,1536]{1,0:T(8,128)(2,1)S(1)}, u32[]{:S(2)}) copy-start(bf16[256,1536]{1,0:T(8,128)(2,1)S(1)} %reshape_reshape.3) | copy-start | bytes 2359300
  59.0 1.2 copy-start.3
  72.5 123.8 %reduce-scatter.12.cloned.1.call-start = ((), (), s32[]{:S(2)}) async-start(), calls=%async_computation.6 | async-start | bytes 4177920
  114.9 1.1 copy-start.1
  114.9 1.6 copy-start.4
  115.0 222.5 %reduce-scatter.8.cloned.1.call-start = ((), (), s32[]{:S(2)}) async-start(), calls=%async_computation.4 | async-start | bytes 16711680 | tf_op jit(solution)/shard_map/reduce_scatter | solution.py:114
  337.5 68.2 %copy-start.6 = (f32[96,2560]{1,0:T(8,128)S(1)}, f32[96,2560]{1,0:T(8,128)}, u32[]{:S(2)}) copy-start(f32[96,2560]{1,0:T(8,128)} %reduce-scatter.8.cloned.1.call-done) | copy-start | bytes 2949124
Sparse Core Ops, SparseCore 0:
  72.6 36.6 reduce-scatter.9
  115.1 81.1 reduce-scatter.11
  200.7 136.7 reduce-scatter.7
